TPU v7x, 512 devices: a whole 4x4x16 slice. The times are simulated.
512 devices in a mesh: seq: 32 (over z, core), dp: 4 (over x), tensor: 4 (over y).
Axes of the slice: x: 4, y: 4, z: 16, core: 2. Of those that a mesh axis runs over, the one named last changes fastest.
Arguments:
- attention_queries: bfloat16 [4, 4096, 3584], P('dp', 'seq', 'tensor')
- attention_keys: bfloat16 [4, 4096, 512], P('dp', 'seq', 'tensor')
- attention_values: bfloat16 [4, 4096, 512], P('dp', 'seq', 'tensor')
- key_window_length: int32 [4], P('tensor'), may hold values from 128 to 512, as said below
- norm_gain: float32 [3584], P('tensor'), may hold values from 0.5 to 2
- spike_levels: int32 [3584], P('tensor'), may hold values from 1 to 4
- lin_queries: bfloat16 [4, 4096, 3584], P('dp', 'seq', 'tensor'), may hold values from -6 to 6
- lin_keys: bfloat16 [4, 4096, 3584], P('dp', 'seq', 'tensor'), may hold values from -6 to 6
- decay_logs: float32 [4, 28, 4096], P('dp', 'tensor', 'seq'), as said below
- cotangent: bfloat16 [4, 4096, 3584], P('dp', 'seq', 'tensor')
Outputs:
- layer_output: bfloat16 [4, 4096, 3584], P('dp', 'seq', 'tensor')
- query_grads: bfloat16 [4, 4096, 3584], P('dp', 'seq', 'tensor')
- key_gradient: bfloat16 [4, 4096, 512], P('dp', 'seq', 'tensor')
- value_gradient: bfloat16 [4, 4096, 512], P('dp', 'seq', 'tensor')
- gain_grads: float32 [3584], P('tensor')
Inputs may be any that keep to these rules, and one draw needn't show every extreme that they name: Key head g lets query t see positions j with t - key_window_length[g] < j <= t; some head has exactly 512. `decay_logs`: non-positive.
All inputs are finite; a program needn't handle non-finite values.
Results may differ from a plain program's by a relative error of at most 0.015.
Values may be sent and summed in bfloat16 or wider, within the bound.
No kernel may reach another device: no remote copies, remote signals or barrier semaphores. Data moves between devices by JAX's collectives and lax.ppermute only.
A program may use at most 128 MiB of HBM per device.

v0:
```python
import math
import jax
import jax.numpy as jnp
from jax import lax
from jax.sharding import PartitionSpec as P

HEAD_SIZE = 128
D = 3584
LONGEST_WINDOW = 512
precise = lax.Precision.HIGHEST
epsilon = 1e-06


def passed_along(block, axis, distance):
    devices = range(lax.axis_size(axis))
    route = [(i - distance, i) for i in devices if i - distance in devices]
    return lax.ppermute(block, axis, route)


def entering(value, axis, join, neutral, backward):
    count, mine = (lax.axis_size(axis), lax.axis_index(axis))
    pieces = jax.tree.map(lambda part: lax.all_gather(part, axis), value)
    if backward:
        pieces = jax.tree.map(lambda part: part[::-1], pieces)
        mine = count - 1 - mine
    running = jax.tree.map(
        lambda part, zero: jnp.full_like(part, 0) + jnp.asarray(zero, part.dtype), value, neutral
    )

    def turn(position, running):
        longer = join(running, jax.tree.map(lambda part: part[position], pieces))
        return jax.tree.map(lambda new, old: jnp.where(position < mine, new, old), longer, running)

    return lax.fori_loop(0, count - 1, turn, running)


def head_logits(query_rows, key_row_block, first_query, key_reach, scaling):
    block_rows = query_rows.shape[0]
    key_span = key_row_block.shape[0] - block_rows
    logits = (
        jnp.einsum("sd,kd->sk", query_rows, key_row_block, preferred_element_type=jnp.float32)
        * scaling
    )
    query_pos = first_query + jnp.arange(block_rows, dtype=jnp.int32)[:, None]
    key_pos = first_query - key_span + jnp.arange(key_row_block.shape[0], dtype=jnp.int32)[None, :]
    allowed = (key_pos >= 0) & (key_pos <= query_pos) & (key_pos > query_pos - key_reach)
    return jnp.where(allowed, logits, -jnp.inf)


def chain_states(earlier, later):
    return (earlier[0] * later[0], later[0][:, None, None] * earlier[1] + later[1])


def local(
    attention_queries,
    attention_keys,
    attention_values,
    key_window_length,
    norm_gain,
    spike_levels,
    lin_queries,
    lin_keys,
    decay_logs,
    cotangent,
):
    block_rows = attention_queries.shape[1]
    q_heads = attention_queries.shape[2] // HEAD_SIZE
    kv_heads = attention_keys.shape[2] // HEAD_SIZE
    head_groups = q_heads // kv_heads
    previous = (LONGEST_WINDOW + block_rows - 1) // block_rows
    key_span = previous * block_rows
    first_query = lax.axis_index("seq") * block_rows
    scaling = 1.0 / math.sqrt(HEAD_SIZE)
    own_pair = jnp.stack([attention_keys, attention_values])
    earlier_blocks = []
    moving = own_pair
    for distance in range(previous):
        moving = passed_along(moving, "seq", 1)
        earlier_blocks.append(moving)
    window_pair = jnp.concatenate(earlier_blocks[::-1] + [own_pair], axis=2)
    window_pair = window_pair.reshape(2, key_span + block_rows, kv_heads, HEAD_SIZE).transpose(
        0, 2, 1, 3
    )
    window_keys = window_pair[0]
    window_values = window_pair[1]
    head_queries = attention_queries[0].reshape(block_rows, q_heads, HEAD_SIZE).transpose(1, 0, 2)
    kv_of_head = jnp.arange(q_heads, dtype=jnp.int32) // head_groups

    def forward_head(operands):
        query_rows, kv_index = operands
        key_row_block = lax.dynamic_index_in_dim(window_keys, kv_index, 0, keepdims=False)
        value_rows = lax.dynamic_index_in_dim(window_values, kv_index, 0, keepdims=False)
        key_reach = lax.dynamic_index_in_dim(key_window_length, kv_index, 0, keepdims=False)
        logits = head_logits(query_rows, key_row_block, first_query, key_reach, scaling)
        row_max = jnp.max(logits, axis=-1)
        exponent = jnp.exp(logits - row_max[:, None])
        row_sum = jnp.sum(exponent, axis=-1)
        weights = (exponent / row_sum[:, None]).astype(jnp.bfloat16)
        head_output = jnp.dot(weights, value_rows, preferred_element_type=jnp.float32).astype(
            jnp.bfloat16
        )
        return (head_output, row_max, row_sum)

    heads_out, maxima, sums = lax.map(forward_head, (head_queries, kv_of_head))
    out_float = heads_out.astype(jnp.float32)
    square_sum = lax.psum(jnp.sum(out_float * out_float, axis=(0, 2)), "tensor")
    inverse = 1.0 / jnp.sqrt(square_sum / D + epsilon)
    normed = out_float * inverse[None, :, None]
    gain_rows = norm_gain.reshape(q_heads, HEAD_SIZE)[:, None, :]
    ceiling = spike_levels.astype(jnp.float32).reshape(q_heads, HEAD_SIZE)[:, None, :]
    bounded = jnp.tanh(normed * gain_rows / ceiling)
    spikes = (ceiling * bounded).astype(jnp.bfloat16)
    membrane_queries = lin_queries[0].reshape(block_rows, q_heads, HEAD_SIZE).transpose(1, 0, 2)
    membrane_keys = lin_keys[0].reshape(block_rows, q_heads, HEAD_SIZE).transpose(1, 0, 2)
    cumulative = jnp.cumsum(decay_logs[0], axis=1)
    lower_mask = jnp.arange(block_rows)[:, None] >= jnp.arange(block_rows)[None, :]
    gaps = jnp.where(lower_mask[None], cumulative[:, :, None] - cumulative[:, None, :], 0.0)
    products = jnp.einsum(
        "hsd,htd->hst", membrane_queries, membrane_keys, preferred_element_type=jnp.float32
    )
    decayed = jnp.where(lower_mask[None], jnp.exp(gaps), 0.0) * products
    spike_float = spikes.astype(jnp.float32)
    query_float = membrane_queries.astype(jnp.float32)
    key_float = membrane_keys.astype(jnp.float32)
    block_decay = jnp.exp(cumulative[:, -1])
    tail_decay = jnp.exp(cumulative[:, -1:] - cumulative)
    local_state = jnp.einsum(
        "hsd,hse->hde", key_float * tail_decay[..., None], spike_float, precision=precise
    )
    identity = (jnp.ones_like(block_decay), jnp.zeros_like(local_state))
    decay_before, state_in = entering(
        (block_decay, local_state), "seq", chain_states, identity, False
    )
    carried = jnp.einsum("hsd,hde->hse", query_float, state_in, precision=precise)
    membrane = (
        jnp.einsum("hst,htd->hsd", decayed, spike_float, precision=precise)
        + jnp.exp(cumulative)[..., None] * carried
    )
    scale_out = 1.0 / jnp.sqrt(jnp.mean(membrane * membrane, axis=-1) + epsilon)
    unit_out = membrane * scale_out[..., None]
    layer_output = (
        unit_out.astype(jnp.bfloat16).transpose(1, 0, 2).reshape(1, block_rows, q_heads * HEAD_SIZE)
    )
    incoming = (
        cotangent[0].reshape(block_rows, q_heads, HEAD_SIZE).transpose(1, 0, 2).astype(jnp.float32)
    )
    membrane_grad = scale_out[..., None] * (
        incoming - unit_out * jnp.mean(incoming * unit_out, axis=-1, keepdims=True)
    )
    head_part = jnp.einsum(
        "hsd,hse->hde",
        query_float * jnp.exp(cumulative)[..., None],
        membrane_grad,
        precision=precise,
    )
    decay_after, state_after = entering(
        (block_decay, head_part), "seq", chain_states, identity, True
    )
    later_part = jnp.einsum("htd,hde->hte", key_float, state_after, precision=precise)
    spike_grad = (
        jnp.einsum("hst,hsd->htd", decayed, membrane_grad, precision=precise)
        + tail_decay[..., None] * later_part
    )
    level_grad = spike_grad * (1.0 - bounded * bounded)
    gain_part = jnp.sum(level_grad * normed, axis=1).reshape(q_heads * HEAD_SIZE)
    gain_grads = lax.psum(gain_part, ("seq", "dp"))
    normed_grad = level_grad * gain_rows
    slope_sum = lax.psum(jnp.sum(normed_grad * normed, axis=(0, 2)), "tensor")
    output_gradient = (
        inverse[None, :, None] * (normed_grad - normed * (slope_sum / D)[None, :, None])
    ).astype(jnp.bfloat16)

    def backward_head(operands):
        query_rows, grad_rows, row_max, row_sum, kv_index = operands
        key_row_block = lax.dynamic_index_in_dim(window_keys, kv_index, 0, keepdims=False)
        value_rows = lax.dynamic_index_in_dim(window_values, kv_index, 0, keepdims=False)
        key_reach = lax.dynamic_index_in_dim(key_window_length, kv_index, 0, keepdims=False)
        logits = head_logits(query_rows, key_row_block, first_query, key_reach, scaling)
        probs = jnp.exp(logits - row_max[:, None]) / row_sum[:, None]
        weights = probs.astype(jnp.bfloat16)
        prob_grad = jnp.einsum(
            "sd,kd->sk", grad_rows, value_rows, preferred_element_type=jnp.float32
        )
        row_delta = jnp.sum(probs * prob_grad, axis=-1, keepdims=True)
        logit_grad = (probs * (prob_grad - row_delta) * scaling).astype(jnp.bfloat16)
        query_grad = jnp.dot(logit_grad, key_row_block, preferred_element_type=jnp.float32)
        key_part = jnp.einsum(
            "sk,sd->kd", logit_grad, query_rows, preferred_element_type=jnp.float32
        )
        value_part = jnp.einsum("sk,sd->kd", weights, grad_rows, preferred_element_type=jnp.float32)
        return (query_grad, key_part, value_part)

    query_parts, key_parts, value_parts = lax.map(
        backward_head, (head_queries, output_gradient, maxima, sums, kv_of_head)
    )
    key_sum = key_parts.reshape(kv_heads, head_groups, key_span + block_rows, HEAD_SIZE).sum(axis=1)
    value_sum = value_parts.reshape(kv_heads, head_groups, key_span + block_rows, HEAD_SIZE).sum(
        axis=1
    )
    pair_grads = jnp.stack([key_sum, value_sum])
    own_grads = pair_grads[:, :, key_span:]
    carried_grads = jnp.zeros_like(own_grads)
    for distance in range(previous, 0, -1):
        offset = (previous - distance) * block_rows
        carried_grads = passed_along(
            carried_grads + pair_grads[:, :, offset : offset + block_rows], "seq", -1
        )
    total_grads = own_grads + carried_grads
    query_grads = (
        query_parts.astype(jnp.bfloat16)
        .transpose(1, 0, 2)
        .reshape(1, block_rows, q_heads * HEAD_SIZE)
    )
    key_gradient = (
        total_grads[0]
        .astype(jnp.bfloat16)
        .transpose(1, 0, 2)
        .reshape(1, block_rows, kv_heads * HEAD_SIZE)
    )
    value_gradient = (
        total_grads[1]
        .astype(jnp.bfloat16)
        .transpose(1, 0, 2)
        .reshape(1, block_rows, kv_heads * HEAD_SIZE)
    )
    return (layer_output, query_grads, key_gradient, value_gradient, gain_grads)


def solution(mesh):
    placed = (
        P("dp", "seq", "tensor"),
        P("dp", "seq", "tensor"),
        P("dp", "seq", "tensor"),
        P("tensor"),
        P("tensor"),
        P("tensor"),
        P("dp", "seq", "tensor"),
        P("dp", "seq", "tensor"),
        P("dp", "tensor", "seq"),
        P("dp", "seq", "tensor"),
    )
    return jax.shard_map(
        local,
        mesh=mesh,
        in_specs=placed,
        out_specs=(
            P("dp", "seq", "tensor"),
            P("dp", "seq", "tensor"),
            P("dp", "seq", "tensor"),
            P("dp", "seq", "tensor"),
            P("tensor"),
        ),
        check_vma=False,
    )
```

profile of v0, /device:TPU:128, one launch (start us, length us, event | category | flops | bytes accessed | tf_op | source)
XLA Modules:
  0.0 720.5 jit_solution(11965284962167923408)
XLA Ops:
  8.0 1.9 collective-permute-start
  10.9 3.9 collective-permute-done
  14.8 1.9 collective-permute-start.1
  16.9 4.7 collective-permute-done.1
  21.6 1.9 collective-permute-start.2
  23.6 4.8 collective-permute-done.2
  28.3 1.9 collective-permute-start.3
  33.4 1.8 collective-permute-done.3
  36.0 28.6 %while.62 = (s32[]{:T(128)}, bf16[7,128,128]{2,1,0:T(8,128)(2,1)S(1)}, f32[7,128]{1,0:T(8,128)}, f32[7,128]{1,0:T(8,128)}, s32[]{:T(128)}, /*index=5*/s32[]{:T(1...) while((s32[]{:T(128)}, ...), condition=%wide.region_4.5_spmd, body=%wide.region_1.4_spmd.sunk | while | flops 42944384 | bytes 1391389 | solution.py:104
  64.8 10.9 %psum.21 = f32[128]{0:T(128)S(1)} all-reduce(f32[128]{0:T(128)S(1)} %fusion.52), channel_id=1, replica_groups=mesh['seq'=32,'dp'=4,'tensor'=4] {'tensor'}, use_global_device_ids=true, to_apply=%region_6.7 | all-reduce | flops 128 | bytes 1024 | tf_op jit(solution)/shard_map/psum | solution.py:106
  79.2 50.1 %all-reduce = f32[224]{0:T(256)S(1)} all-reduce(f32[224]{0:T(256)S(1)} %dynamic-update-slice), channel_id=2, replica_groups=mesh['seq'=32,'dp'=4,'tensor'=4] {'seq'}, use_global_device_ids=true, to_apply=%add | all-reduce | flops 224 | bytes 1792
  130.1 41.7 %all-gather.6.cloned.1.call-done = f32[224,128,128]{2,1,0:T(8,128)} async-done(((f32[7,128,128]{2,1,0:T(8,128)}), f32[224,128,128]{2,1,0:T(8,128)}) %all-gather.6.cloned.1.call-update) | async-done | bytes 14680080 | tf_op jit(solution)/shard_map/all_gather | solution.py:22
  171.8 36.8 %while.64 = (s32[]{:T(128)}, f32[7,128,128]{2,1,0:T(8,128)S(1)}, s32[]{:T(128)}, f32[32,7]{1,0:T(8,128)S(1)}, f32[32,7,128,128]{3,2,1,0:T(8,128)}, /*index=5*/s32[]{:T(128)}, s32[]{:T(128)}) while((s32[]{:T(128)}, f32[7,128,128]{2,1,0:T(8,128)S(1)}, s32[]{:T(128)}, f32[32,7]{1,0:T(8,128)S(1)}, f32[32,7,128,128]{3,2,1,0:T(8,128)}, ...), condition=%wide.region_8.9_spmd.clone, body=%wide.region_7.8_spmd.clone.sunk | while | flops 458756 | bytes 1376453 | solution.py:34
  211.6 1.9 fusion.56
  214.1 93.6 %all-gather.8.cloned.1.call-done = f32[224,128,128]{2,1,0:T(8,128)} async-done(((f32[7,128,128]{2,1,0:T(8,128)}), f32[224,128,128]{2,1,0:T(8,128)}) %all-gather.8.cloned.1.call-update) | async-done | bytes 14680080 | tf_op jit(solution)/shard_map/all_gather | solution.py:22
  307.7 13.1 %rev.7 = f32[32,7,128,128]{3,2,1,0:T(8,128)} reverse(f32[32,7,128,128]{3,2,1,0:T(8,128)} %bitcast.189), dimensions={0} | reverse | bytes 29360128 | tf_op jit(solution)/shard_map/rev | solution.py:24
  320.8 57.7 %while.65 = (s32[]{:T(128)}, f32[7,128,128]{2,1,0:T(8,128)S(1)}, s32[]{:T(128)}, f32[32,7]{1,0:T(8,128)}, f32[32,7,128,128]{3,2,1,0:T(8,128)}, /*index=5*/s32[]{:T(128)}, s32[]{:T(128)}) while((s32[]{:T(128)}, f32[7,128,128]{2,1,0:T(8,128)S(1)}, s32[]{:T(128)}, f32[32,7]{1,0:T(8,128)}, f32[32,7,128,128]{3,2,1,0:T(8,128)}, ...), condition=%wide.region_12.13_spmd.clone, body=%wide.region_11.12_spmd.clone.sunk | while | flops 458756 | bytes 1376453 | solution.py:34
  379.9 3.7 fusion.51
  383.5 10.4 %psum.22 = f32[128]{0:T(128)S(1)} all-reduce(f32[128]{0:T(128)S(1)} %get-tuple-element.606), channel_id=1, replica_groups=mesh['seq'=32,'dp'=4,'tensor'=4] {'tensor'}, use_global_device_ids=true, to_apply=%region_14.15 | all-reduce | flops 128 | bytes 1024 | tf_op jit(solution)/shard_map/psum | solution.py:168
  395.2 39.9 %while.63 = (s32[]{:T(128)}, bf16[7,128,128]{1,2,0:T(8,128)(2,1)}, f32[7,640,128]{2,1,0:T(8,128)}, f32[7,640,128]{2,1,0:T(8,128)S(1)}, s32[]{:T(128)}, /*index=5...) while((s32[]{:T(128)}, bf16[7,128,128]{1,2,0:T(8,128)(2,1)}, ...), condition=%wide.region_17.18_spmd, body=%wide.region_15.17_spmd.sunk | while | flops 106088448 | bytes 3815853 | solution.py:193
  399.2 1.7 fusion.121
  404.9 1.8 fusion.121
  410.6 1.7 fusion.121
  435.3 1.8 reduce_sum.91
  437.2 2.1 collective-permute-start.4
  439.2 2.5 collective-permute-done.4
  441.7 5.0 collective-permute-start.5
  446.7 2.5 collective-permute-done.5
  449.2 5.0 collective-permute-start.6
  454.2 2.5 collective-permute-done.6
  456.8 5.0 collective-permute-start.7
  463.5 249.5 %psum.23 = f32[896]{0:T(1024)} all-reduce(f32[896]{0:T(1024)S(1)} %bitcast.224), channel_id=1, replica_groups=mesh['seq'=32,'dp'=4,'tensor'=4] {'seq','dp'}, use_global_device_ids=true, to_apply=%region_21.22 | all-reduce | flops 896 | bytes 7168 | tf_op jit(solution)/shard_map/psum | solution.py:166
  (339 shorter events, 174.0 us)
Async XLA Ops:
  7.2 164.7 %all-gather.6.cloned.1.call-start = ((), (), s32[]{:S(2)}) async-start(), calls=%async_computation | async-start | bytes 15138816 | tf_op jit(solution)/shard_map/all_gather | solution.py:22
  8.0 6.8 collective-permute-start
  14.8 6.8 collective-permute-start.1
  21.6 6.8 collective-permute-start.2
  23.5 52.1 %copy-start.11 = (f32[7,128]{1,0:T(8,128)}, f32[7,128]{1,0:T(8,128)S(1)}, u32[]{:S(2)}) copy-start(f32[7,128]{1,0:T(8,128)S(1)} %get-tuple-element.695) | copy-start | bytes 10756
  28.3 6.8 collective-permute-start.3
  31.0 178.2 %copy-start.13 = (f32[7,128]{1,0:T(8,128)}, f32[7,128]{1,0:T(8,128)S(1)}, u32[]{:S(2)}) copy-start(f32[7,128]{1,0:T(8,128)S(1)} %convert_bitcast_fusion) | copy-start | bytes 10756
  33.4 96.4 %copy-start.5 = (bf16[1,128,896]{1,2,0:T(8,128)(2,1)}, bf16[1,128,896]{1,2,0:T(8,128)(2,1)S(1)}, u32[]{:S(2)}) copy-start(bf16[1,128,896]{1,2,0:T(8,128)(2,1)S(1)} %copy.51) | copy-start | bytes 688132
  36.0 39.6 %copy-start.12 = (f32[896]{0:T(1024)S(1)}, f32[896]{0:T(1024)}, u32[]{:S(2)}) copy-start(f32[896]{0:T(1024)} %param.22) | copy-start | bytes 10756
  64.6 64.8 %copy-start.6 = (bf16[7,128,128]{2,1,0:T(8,128)(2,1)}, bf16[7,128,128]{2,1,0:T(8,128)(2,1)S(1)}, u32[]{:S(2)}) copy-start(bf16[7,128,128]{2,1,0:T(8,128)(2,1)S(1)} %get-tuple-element.1047) | copy-start | bytes 688132
  64.6 144.6 %copy-start.3 = (bf16[7,128,128]{2,1,0:T(8,128)(2,1)}, bf16[7,128,128]{2,1,0:T(8,128)(2,1)S(1)}, u32[]{:S(2)}) copy-start(bf16[7,128,128]{2,1,0:T(8,128)(2,1)S(1)} %get-tuple-element.500) | copy-start | bytes 688132
  64.6 64.8 %copy-start.8 = (bf16[1,128,896]{2,1,0:T(8,128)(2,1)S(1)}, bf16[1,128,896]{2,1,0:T(8,128)(2,1)}, u32[]{:S(2)}) copy-start(bf16[1,128,896]{2,1,0:T(8,128)(2,1)} %param.24) | copy-start | bytes 688132
  64.6 65.0 %copy-start.10 = (bf16[1,128,896]{2,1,0:T(8,128)(2,1)S(1)}, bf16[1,128,896]{2,1,0:T(8,128)(2,1)}, u32[]{:S(2)}) copy-start(bf16[1,128,896]{2,1,0:T(8,128)(2,1)} %param.27) | copy-start | bytes 688132
  75.6 133.6 %copy-start.15 = (f32[128]{0:T(128)}, f32[128]{0:T(128)S(1)}, u32[]{:S(2)}) copy-start(f32[128]{0:T(128)S(1)} %add_rsqrt_fusion.1) | copy-start | bytes 1540
  77.0 230.7 %all-gather.8.cloned.1.call-start = ((), (), s32[]{:S(2)}) async-start(), calls=%async_computation.1 | async-start | bytes 15138816 | tf_op jit(solution)/shard_map/all_gather | solution.py:22
  130.1 79.1 %copy-start.16 = (f32[7,128,128]{2,1,0:T(8,128)}, f32[7,128,128]{2,1,0:T(8,128)S(1)}, u32[]{:S(2)}) copy-start(f32[7,128,128]{2,1,0:T(8,128)S(1)} %convolution_multiply_fusion.3) | copy-start | bytes 1376260
  209.2 0.8 copy-start
  211.5 2.6 copy-start.2
  379.9 14.1 %copy-start.4 = (bf16[7,128,128]{2,1,0:T(8,128)(2,1)S(1)}, bf16[7,128,128]{2,1,0:T(8,128)(2,1)}, u32[]{:S(2)}) copy-start(bf16[7,128,128]{2,1,0:T(8,128)(2,1)} %copy-done.3) | copy-start | bytes 688132
  437.1 24.7 %copy-start.1 = (f32[7,128,128]{2,1,0:T(8,128)S(1)}, f32[7,128,128]{2,1,0:T(8,128)}, u32[]{:S(2)}) copy-start(f32[7,128,128]{2,1,0:T(8,128)} %copy-done) | copy-start | bytes 1376260
  437.1 24.7 %copy-start.7 = (f32[7,128,128]{1,2,0:T(8,128)S(1)}, f32[7,128,128]{1,2,0:T(8,128)}, u32[]{:S(2)}) copy-start(f32[7,128,128]{1,2,0:T(8,128)} %get-tuple-element.696) | copy-start | bytes 1376260
  437.1 25.6 %copy-start.9 = (bf16[7,128,128]{1,2,0:T(8,128)(2,1)S(1)}, bf16[7,128,128]{1,2,0:T(8,128)(2,1)}, u32[]{:S(2)}) copy-start(bf16[7,128,128]{1,2,0:T(8,128)(2,1)} %get-tuple-element.505) | copy-start | bytes 688132
  437.1 26.4 %copy-start.14 = (f32[7,128]{1,0:T(8,128)S(1)}, f32[7,128]{1,0:T(8,128)}, u32[]{:S(2)}) copy-start(f32[7,128]{1,0:T(8,128)} %get-tuple-element.605) | copy-start | bytes 10756
  437.2 4.6 collective-permute-start.4
  441.7 7.5 %collective-permute-start.5 = (f32[2,1,128,128]{3,2,1,0:T(8,128)S(1)}, f32[2,1,128,128]{3,2,1,0:T(8,128)S(1)}, u32[]{:S(2)}, u32[]{:S(2)}) collective-permute-start(f32[2,1,128,128]{3,2,1,0:T(8,128)S(1)} %fusion.71), channel_id=1, source_target_pairs={{16,0},{32,16},{48,32},{64,48},{80,64},{96,80},{112,96},{128,112},... | collective-permute-start | bytes 393224 | tf_op jit(solution)/shard_map/ppermute | solution.py:17
  449.2 7.5 %collective-permute-start.6 = (f32[2,1,128,128]{3,2,1,0:T(8,128)S(1)}, f32[2,1,128,128]{3,2,1,0:T(8,128)S(1)}, u32[]{:S(2)}, u32[]{:S(2)}) collective-permute-start(f32[2,1,128,128]{3,2,1,0:T(8,128)S(1)} %fusion.65), channel_id=1, source_target_pairs={{16,0},{32,16},{48,32},{64,48},{80,64},{96,80},{112,96},{128,112},... | collective-permute-start | bytes 393224 | tf_op jit(solution)/shard_map/ppermute | solution.py:17
  456.8 256.3 %collective-permute-start.7 = (f32[2,1,128,128]{3,2,1,0:T(8,128)S(1)}, f32[2,1,128,128]{3,2,1,0:T(8,128)S(1)}, u32[]{:S(2)}, u32[]{:S(2)}) collective-permute-start(f32[2,1,128,128]{3,2,1,0:T(8,128)S(1)} %fusion.72), channel_id=1, source_target_pairs={{16,0},{32,16},{48,32},{64,48},{80,64},{96,80},{112,96},{128,112},... | collective-permute-start | bytes 393224 | tf_op jit(solution)/shard_map/ppermute | solution.py:17
Sparse Core Ops, SparseCore 0:
  77.1 94.7 all-gather.5
  213.6 94.0 all-gather.7
where the time goes:
time: 727 us; the launch traced here: 721 us
  blocking collectives  321 us (44%)
  waiting for transfers between devices  158 us (22%)
  other arithmetic  88.5 us (12%)
  local copies, waits for them, and re-layouts  67 us (9%)
  matrix products  44.1 us (6%)
  starting transfers between devices  24.7 us (3%)
  between operations  15.1 us (2%)
    psum x1, blocking collectives, local(): gain_grads = lax.psum(gain_part, ('seq', 'dp'))  250 us
    all_gather x2, waiting for transfers between devices, entering(): pieces = jax.tree.map(lambda part: lax.all_gather(part, axis), value)  135 us
    select_n x62, other arithmetic, turn(): jnp.where(position < mine, new, old)  70.8 us
    unnamed x1, blocking collectives  50.1 us
    ppermute x8, starting transfers between devices, passed_along(): return lax.ppermute(block, axis, route)  24.7 us
    ppermute x8, waiting for transfers between devices, passed_along(): return lax.ppermute(block, axis, route)  22.6 us
    mul x62, local copies, waits for them, and re-layouts, chain_states(): later[0][:, None, None] * earlier[1] + later[1]  21.9 us
    dynamic_update_slice x14, local copies, waits for them, and re-layouts, local(): heads_out, maxima, sums = lax.map(forward_head, (head_queries, kv_of_head))  18.1 us
  transfers between devices with their start and end apart: 10, of which 9 were waited for; matrix products, arithmetic and copies ran while one was open for 1% of the time, Pallas kernels for 0%

commit v1 on v0

--- a/solution.py
+++ b/solution.py
@@ -1,3 +1,4 @@
+import functools
 import math
 import jax
 import jax.numpy as jnp
@@ -9,6 +10,14 @@
 LONGEST_WINDOW = 512
 precise = lax.Precision.HIGHEST
 epsilon = 1e-06
+
+
+def corner_read(packet, a_name):
+    arr_next = jax.lax.all_gather(packet, axis_name=a_name)
+    return jnp.sum(arr_next, axis=0)
+
+
+lift_the_local_data = functools.partial(corner_read, a_name=("seq", "dp"))
 
 
 def passed_along(block, axis, distance):
@@ -163,7 +172,7 @@
     )
     level_grad = spike_grad * (1.0 - bounded * bounded)
     gain_part = jnp.sum(level_grad * normed, axis=1).reshape(q_heads * HEAD_SIZE)
-    gain_grads = lax.psum(gain_part, ("seq", "dp"))
+    gain_grads = lift_the_local_data(gain_part)
     normed_grad = level_grad * gain_rows
     slope_sum = lax.psum(jnp.sum(normed_grad * normed, axis=(0, 2)), "tensor")
     output_gradient = (

time: 727 us -> 621 us (0.85)
  the two profiles are of different devices: /device:TPU:128 before, /device:TPU:97 now
where the time goes in v1:
time: 621 us; the launch traced here: 615 us
  blocking collectives  210 us (34%)
  waiting for transfers between devices  155 us (25%)
  other arithmetic  89.5 us (14%)
  local copies, waits for them, and re-layouts  67 us (11%)
  matrix products  44.1 us (7%)
  starting transfers between devices  32 us (5%)
  between operations  15.1 us (2%)
    all_gather x1, blocking collectives, corner_read(): arr_next = jax.lax.all_gather(packet, axis_name=a_name)  142 us
    all_gather x2, waiting for transfers between devices, entering(): pieces = jax.tree.map(lambda part: lax.all_gather(part, axis), value)  137 us
    select_n x62, other arithmetic, turn(): jnp.where(position < mine, new, old)  70.8 us
    unnamed x1, blocking collectives  50.3 us
    ppermute x8, starting transfers between devices, passed_along(): return lax.ppermute(block, axis, route)  31.9 us
    mul x62, local copies, waits for them, and re-layouts, chain_states(): later[0][:, None, None] * earlier[1] + later[1]  21.9 us
    dynamic_update_slice x14, local copies, waits for them, and re-layouts, local(): heads_out, maxima, sums = lax.map(forward_head, (head_queries, kv_of_head))  18.1 us
    ppermute x8, waiting for transfers between devices, passed_along(): return lax.ppermute(block, axis, route)  17.6 us
  transfers between devices with their start and end apart: 10, of which 8 were waited for; matrix products, arithmetic and copies ran while one was open for 2% of the time, Pallas kernels for 0%

profile of v1, /device:TPU:97, one launch (start us, length us, event | category | flops | bytes accessed | tf_op | source)
XLA Modules:
  0.0 614.7 jit_solution(16341887338407245856)
XLA Ops:
  8.0 5.3 collective-permute-start
  14.6 5.5 collective-permute-start.1
  21.4 5.5 collective-permute-start.2
  28.2 5.5 collective-permute-start.3
  37.7 28.6 %while.62 = (s32[]{:T(128)}, bf16[7,128,128]{2,1,0:T(8,128)(2,1)S(1)}, f32[7,128]{1,0:T(8,128)}, f32[7,128]{1,0:T(8,128)}, s32[]{:T(128)}, /*index=5*/s32[]{:T(1...) while((s32[]{:T(128)}, ...), condition=%wide.region_4.5_spmd, body=%wide.region_1.4_spmd.sunk | while | flops 42944384 | bytes 1391389 | solution.py:113
  66.4 8.9 %psum.14 = f32[128]{0:T(128)S(1)} all-reduce(f32[128]{0:T(128)S(1)} %fusion.52), channel_id=1, replica_groups=mesh['seq'=32,'dp'=4,'tensor'=4] {'tensor'}, use_global_device_ids=true, to_apply=%region_6.7 | all-reduce | flops 128 | bytes 1024 | tf_op jit(solution)/shard_map/psum | solution.py:115
  78.9 50.3 %all-reduce = f32[224]{0:T(256)S(1)} all-reduce(f32[224]{0:T(256)S(1)} %dynamic-update-slice), channel_id=2, replica_groups=mesh['seq'=32,'dp'=4,'tensor'=4] {'seq'}, use_global_device_ids=true, to_apply=%add | all-reduce | flops 224 | bytes 1792
  130.0 43.8 %all-gather.7.cloned.1.call-done = f32[224,128,128]{2,1,0:T(8,128)} async-done(((f32[7,128,128]{2,1,0:T(8,128)}), f32[224,128,128]{2,1,0:T(8,128)}) %all-gather.7.cloned.1.call-update) | async-done | bytes 14680080 | tf_op jit(solution)/shard_map/all_gather | solution.py:31
  173.8 36.8 %while.64 = (s32[]{:T(128)}, f32[7,128,128]{2,1,0:T(8,128)S(1)}, s32[]{:T(128)}, f32[32,7]{1,0:T(8,128)S(1)}, f32[32,7,128,128]{3,2,1,0:T(8,128)}, /*index=5*/s32[]{:T(128)}, s32[]{:T(128)}) while((s32[]{:T(128)}, f32[7,128,128]{2,1,0:T(8,128)S(1)}, s32[]{:T(128)}, f32[32,7]{1,0:T(8,128)S(1)}, f32[32,7,128,128]{3,2,1,0:T(8,128)}, ...), condition=%wide.region_8.9_spmd.clone, body=%wide.region_7.8_spmd.clone.sunk | while | flops 458756 | bytes 1376453 | solution.py:43
  213.6 1.9 fusion.56
  216.1 93.6 %all-gather.9.cloned.1.call-done = f32[224,128,128]{2,1,0:T(8,128)} async-done(((f32[7,128,128]{2,1,0:T(8,128)}), f32[224,128,128]{2,1,0:T(8,128)}) %all-gather.9.cloned.1.call-update) | async-done | bytes 14680080 | tf_op jit(solution)/shard_map/all_gather | solution.py:31
  309.7 13.1 %rev.7 = f32[32,7,128,128]{3,2,1,0:T(8,128)} reverse(f32[32,7,128,128]{3,2,1,0:T(8,128)} %bitcast.188), dimensions={0} | reverse | bytes 29360128 | tf_op jit(solution)/shard_map/rev | solution.py:33
  322.8 57.7 %while.65 = (s32[]{:T(128)}, f32[7,128,128]{2,1,0:T(8,128)S(1)}, s32[]{:T(128)}, f32[32,7]{1,0:T(8,128)}, f32[32,7,128,128]{3,2,1,0:T(8,128)}, /*index=5*/s32[]{:T(128)}, s32[]{:T(128)}) while((s32[]{:T(128)}, f32[7,128,128]{2,1,0:T(8,128)S(1)}, s32[]{:T(128)}, f32[32,7]{1,0:T(8,128)}, f32[32,7,128,128]{3,2,1,0:T(8,128)}, ...), condition=%wide.region_12.13_spmd.clone, body=%wide.region_11.12_spmd.clone.sunk | while | flops 458756 | bytes 1376453 | solution.py:43
  381.8 3.7 fusion.51
  385.5 8.4 %psum.15 = f32[128]{0:T(128)S(1)} all-reduce(f32[128]{0:T(128)S(1)} %get-tuple-element.606), channel_id=1, replica_groups=mesh['seq'=32,'dp'=4,'tensor'=4] {'tensor'}, use_global_device_ids=true, to_apply=%region_14.15 | all-reduce | flops 128 | bytes 1024 | tf_op jit(solution)/shard_map/psum | solution.py:177
  395.2 39.9 %while.63 = (s32[]{:T(128)}, bf16[7,128,128]{1,2,0:T(8,128)(2,1)}, f32[7,640,128]{2,1,0:T(8,128)}, f32[7,640,128]{2,1,0:T(8,128)S(1)}, s32[]{:T(128)}, /*index=5...) while((s32[]{:T(128)}, bf16[7,128,128]{1,2,0:T(8,128)(2,1)}, ...), condition=%wide.region_17.18_spmd, body=%wide.region_15.17_spmd.sunk | while | flops 106088448 | bytes 3815853 | solution.py:202
  399.1 1.7 fusion.121
  404.9 1.8 fusion.121
  410.6 1.7 fusion.121
  416.3 1.7 fusion.121
  422.0 1.7 fusion.121
  427.7 1.7 fusion.121
  433.4 1.7 fusion.121
  435.2 1.8 reduce_sum.100
  437.1 4.3 collective-permute-start.4
  441.4 3.8 collective-permute-done.4
  445.3 2.1 collective-permute-start.5
  447.3 5.6 collective-permute-done.5
  452.9 1.9 collective-permute-start.6
  454.8 5.6 collective-permute-done.6
  460.4 1.9 collective-permute-start.7
  463.3 142.1 %all-gather.3 = f32[128,1,896]{2,1,0:T(1,128)S(1)} all-gather(f32[1,1,896]{2,1,0:T(1,128)S(1)} %reshape.161), channel_id=1, replica_groups=mesh['seq'=32,'dp'=4,'tensor'=4] {'seq','dp'}, dimensions={0}, use_global_device_ids=true | all-gather | bytes 462336 | tf_op jit(solution)/shard_map/all_gather | solution.py:16
  (341 shorter events, 170.8 us)
Async XLA Ops:
  7.2 166.7 %all-gather.7.cloned.1.call-start = ((), (), s32[]{:S(2)}) async-start(), calls=%async_computation | async-start | bytes 15138816 | tf_op jit(solution)/shard_map/all_gather | solution.py:31
  8.0 6.6 %collective-permute-start = (bf16[2,1,128,128]{3,2,1,0:T(8,128)(2,1)S(1)}, bf16[2,1,128,128]{3,2,1,0:T(8,128)(2,1)S(1)}, u32[]{:S(2)}, u32[]{:S(2)}) collective-permute-start(bf16[2,1,128,128]{3,2,1,0:T(8,128)(2,1)S(1)} %pad_maximum_fusion.1), channel_id=1, source_target_pairs={{0,16},{16,32},{32,48},{48,64},{64,80},{80,96},{96,112},{112,128},... | collective-permute-start | bytes 196616 | tf_op jit(solution)/shard_map/ppermute | solution.py:26
  14.6 6.8 %collective-permute-start.1 = (bf16[2,1,128,128]{3,2,1,0:T(8,128)(2,1)S(1)}, bf16[2,1,128,128]{3,2,1,0:T(8,128)(2,1)S(1)}, u32[]{:S(2)}, u32[]{:S(2)}) collective-permute-start(bf16[2,1,128,128]{3,2,1,0:T(8,128)(2,1)S(1)} %collective-permute-done), channel_id=1, source_target_pairs={{0,16},{16,32},{32,48},{48,64},{64,80},{80,96},{96,112},{112,128},... | collective-permute-start | bytes 196616 | tf_op jit(solution)/shard_map/ppermute | solution.py:26
  21.4 6.8 %collective-permute-start.2 = (bf16[2,1,128,128]{3,2,1,0:T(8,128)(2,1)S(1)}, bf16[2,1,128,128]{3,2,1,0:T(8,128)(2,1)S(1)}, u32[]{:S(2)}, u32[]{:S(2)}) collective-permute-start(bf16[2,1,128,128]{3,2,1,0:T(8,128)(2,1)S(1)} %collective-permute-done.1), channel_id=1, source_target_pairs={{0,16},{16,32},{32,48},{48,64},{64,80},{80,96},{96,112},{112,128},... | collective-permute-start | bytes 196616 | tf_op jit(solution)/shard_map/ppermute | solution.py:26
  26.9 48.3 %copy-start.11 = (f32[7,128]{1,0:T(8,128)}, f32[7,128]{1,0:T(8,128)S(1)}, u32[]{:S(2)}) copy-start(f32[7,128]{1,0:T(8,128)S(1)} %get-tuple-element.695) | copy-start | bytes 10756
  28.2 8.6 %collective-permute-start.3 = (bf16[2,1,128,128]{3,2,1,0:T(8,128)(2,1)S(1)}, bf16[2,1,128,128]{3,2,1,0:T(8,128)(2,1)S(1)}, u32[]{:S(2)}, u32[]{:S(2)}) collective-permute-start(bf16[2,1,128,128]{3,2,1,0:T(8,128)(2,1)S(1)} %collective-permute-done.2), channel_id=1, source_target_pairs={{0,16},{16,32},{32,48},{48,64},{64,80},{80,96},{96,112},{112,128},... | collective-permute-start | bytes 196616 | tf_op jit(solution)/shard_map/ppermute | solution.py:26
  34.4 176.8 %copy-start.13 = (f32[7,128]{1,0:T(8,128)}, f32[7,128]{1,0:T(8,128)S(1)}, u32[]{:S(2)}) copy-start(f32[7,128]{1,0:T(8,128)S(1)} %convert_bitcast_fusion) | copy-start | bytes 10756
  36.8 92.9 %copy-start.5 = (bf16[1,128,896]{1,2,0:T(8,128)(2,1)}, bf16[1,128,896]{1,2,0:T(8,128)(2,1)S(1)}, u32[]{:S(2)}) copy-start(bf16[1,128,896]{1,2,0:T(8,128)(2,1)S(1)} %copy.51) | copy-start | bytes 688132
  37.7 37.6 %copy-start.12 = (f32[896]{0:T(1024)S(1)}, f32[896]{0:T(1024)}, u32[]{:S(2)}) copy-start(f32[896]{0:T(1024)} %param.22) | copy-start | bytes 10756
  66.3 63.0 %copy-start.6 = (bf16[7,128,128]{2,1,0:T(8,128)(2,1)}, bf16[7,128,128]{2,1,0:T(8,128)(2,1)S(1)}, u32[]{:S(2)}) copy-start(bf16[7,128,128]{2,1,0:T(8,128)(2,1)S(1)} %get-tuple-element.1047) | copy-start | bytes 688132
  66.3 144.9 %copy-start.3 = (bf16[7,128,128]{2,1,0:T(8,128)(2,1)}, bf16[7,128,128]{2,1,0:T(8,128)(2,1)S(1)}, u32[]{:S(2)}) copy-start(bf16[7,128,128]{2,1,0:T(8,128)(2,1)S(1)} %get-tuple-element.500) | copy-start | bytes 688132
  66.3 63.0 %copy-start.8 = (bf16[1,128,896]{2,1,0:T(8,128)(2,1)S(1)}, bf16[1,128,896]{2,1,0:T(8,128)(2,1)}, u32[]{:S(2)}) copy-start(bf16[1,128,896]{2,1,0:T(8,128)(2,1)} %param.24) | copy-start | bytes 688132
  66.3 63.2 %copy-start.10 = (bf16[1,128,896]{2,1,0:T(8,128)(2,1)S(1)}, bf16[1,128,896]{2,1,0:T(8,128)(2,1)}, u32[]{:S(2)}) copy-start(bf16[1,128,896]{2,1,0:T(8,128)(2,1)} %param.27) | copy-start | bytes 688132
  75.3 135.9 %copy-start.15 = (f32[128]{0:T(128)}, f32[128]{0:T(128)S(1)}, u32[]{:S(2)}) copy-start(f32[128]{0:T(128)S(1)} %add_rsqrt_fusion.1) | copy-start | bytes 1540
  76.6 233.0 %all-gather.9.cloned.1.call-start = ((), (), s32[]{:S(2)}) async-start(), calls=%async_computation.1 | async-start | bytes 15138816 | tf_op jit(solution)/shard_map/all_gather | solution.py:31
  130.0 81.2 %copy-start.16 = (f32[7,128,128]{2,1,0:T(8,128)}, f32[7,128,128]{2,1,0:T(8,128)S(1)}, u32[]{:S(2)}) copy-start(f32[7,128,128]{2,1,0:T(8,128)S(1)} %convolution_multiply_fusion.3) | copy-start | bytes 1376260
  211.2 0.8 copy-start
  213.5 2.6 copy-start.2
  381.8 12.1 %copy-start.4 = (bf16[7,128,128]{2,1,0:T(8,128)(2,1)S(1)}, bf16[7,128,128]{2,1,0:T(8,128)(2,1)}, u32[]{:S(2)}) copy-start(bf16[7,128,128]{2,1,0:T(8,128)(2,1)} %copy-done.3) | copy-start | bytes 688132
  437.0 25.3 %copy-start.1 = (f32[7,128,128]{2,1,0:T(8,128)S(1)}, f32[7,128,128]{2,1,0:T(8,128)}, u32[]{:S(2)}) copy-start(f32[7,128,128]{2,1,0:T(8,128)} %copy-done) | copy-start | bytes 1376260
  437.0 25.3 %copy-start.7 = (f32[7,128,128]{1,2,0:T(8,128)S(1)}, f32[7,128,128]{1,2,0:T(8,128)}, u32[]{:S(2)}) copy-start(f32[7,128,128]{1,2,0:T(8,128)} %get-tuple-element.696) | copy-start | bytes 1376260
  437.1 26.2 %copy-start.14 = (f32[7,128]{1,0:T(8,128)S(1)}, f32[7,128]{1,0:T(8,128)}, u32[]{:S(2)}) copy-start(f32[7,128]{1,0:T(8,128)} %get-tuple-element.605) | copy-start | bytes 10756
  437.1 8.1 %collective-permute-start.4 = (f32[2,1,128,128]{3,2,1,0:T(8,128)S(1)}, f32[2,1,128,128]{3,2,1,0:T(8,128)S(1)}, u32[]{:S(2)}, u32[]{:S(2)}) collective-permute-start(f32[2,1,128,128]{3,2,1,0:T(8,128)S(1)} %fusion.69), channel_id=1, source_target_pairs={{16,0},{32,16},{48,32},{64,48},{80,64},{96,80},{112,96},{128,112},... | collective-permute-start | bytes 393224 | tf_op jit(solution)/shard_map/ppermute | solution.py:26
  445.3 161.1 %copy-start.9 = (bf16[7,128,128]{1,2,0:T(8,128)(2,1)S(1)}, bf16[7,128,128]{1,2,0:T(8,128)(2,1)}, u32[]{:S(2)}) copy-start(bf16[7,128,128]{1,2,0:T(8,128)(2,1)} %get-tuple-element.505) | copy-start | bytes 688132
  445.3 7.6 %collective-permute-start.5 = (f32[2,1,128,128]{3,2,1,0:T(8,128)S(1)}, f32[2,1,128,128]{3,2,1,0:T(8,128)S(1)}, u32[]{:S(2)}, u32[]{:S(2)}) collective-permute-start(f32[2,1,128,128]{3,2,1,0:T(8,128)S(1)} %fusion.71), channel_id=1, source_target_pairs={{16,0},{32,16},{48,32},{64,48},{80,64},{96,80},{112,96},{128,112},... | collective-permute-start | bytes 393224 | tf_op jit(solution)/shard_map/ppermute | solution.py:26
  452.9 7.5 %collective-permute-start.6 = (f32[2,1,128,128]{3,2,1,0:T(8,128)S(1)}, f32[2,1,128,128]{3,2,1,0:T(8,128)S(1)}, u32[]{:S(2)}, u32[]{:S(2)}) collective-permute-start(f32[2,1,128,128]{3,2,1,0:T(8,128)S(1)} %fusion.65), channel_id=1, source_target_pairs={{16,0},{32,16},{48,32},{64,48},{80,64},{96,80},{112,96},{128,112},... | collective-permute-start | bytes 393224 | tf_op jit(solution)/shard_map/ppermute | solution.py:26
  460.4 146.8 %collective-permute-start.7 = (f32[2,1,128,128]{3,2,1,0:T(8,128)S(1)}, f32[2,1,128,128]{3,2,1,0:T(8,128)S(1)}, u32[]{:S(2)}, u32[]{:S(2)}) collective-permute-start(f32[2,1,128,128]{3,2,1,0:T(8,128)S(1)} %fusion.72), channel_id=1, source_target_pairs={{16,0},{32,16},{48,32},{64,48},{80,64},{96,80},{112,96},{128,112},... | collective-permute-start | bytes 393224 | tf_op jit(solution)/shard_map/ppermute | solution.py:26
Sparse Core Ops, SparseCore 0:
  76.7 97.0 all-gather.6
  215.6 94.0 all-gather.8
